TPU v7x, 512 devices: a whole 4x8x8 slice. The times are simulated.
512 devices in a mesh: space: 32 (over y, x_lo, core), modes: 16 (over z, x_hi).
Axes of the slice: x: 4 (x_hi: 2, x_lo: 2; x = x_hi * 2 + x_lo), y: 8, z: 8, core: 2. Of those that a mesh axis runs over, the one named last changes fastest.
Arguments:
- rhs: bfloat16 [2, 256, 512, 512], P(None, 'modes', 'space'), may hold values from -6 to 6
- initial: bfloat16 [2, 256, 512, 512], P(None, 'modes', 'space'), may hold values from -6 to 6
- region: int32 [512, 512], P('space'), may hold values from 0 to 7
- base_table: float32 [2, 8], replicated, may hold values from 0.5 to 4
- term_table: float32 [2, 3, 8], replicated, may hold values from -0.3 to 0.3
- galerkin: bfloat16 [3, 256, 256], replicated, may hold values from -0.375 to 0.375
- block_mask: int32 [3, 16, 16], replicated, may hold values from 0 to 1, as said below
- block_inverse: float32 [16, 16, 16], P('modes'), as said below
Outputs:
- solution: float32 [2, 256, 512, 512], P(None, 'modes', 'space')
Inputs may be any that keep to these rules, and one draw needn't show every extreme that they name: `block_mask`: each mode block is coupled with itself by every term, and some pairs of mode blocks are not coupled. `block_inverse`: blocks near the identity, off-diagonal entries at most 0.3 in magnitude.
All inputs are finite; a program needn't handle non-finite values.
Results may differ from a plain program's by a relative error of at most 0.0017.
Values may be sent and summed in bfloat16 or wider, within the bound.
No kernel may reach another device: no remote copies, remote signals or barrier semaphores. Data moves between devices by JAX's collectives and lax.ppermute only.
A program may use at most 64 MiB of HBM per device.

v0:
```python
import jax
import jax.numpy as jnp
from jax import lax
from jax.sharding import PartitionSpec as P

SWEEPS = 2


def with_halo(block, sides, width):
    for axis, dim in sides:
        count = lax.axis_size(axis)
        forward = [(i, i + 1) for i in range(count - 1)]
        forward.append((count - 1, 0))
        backward = [(target, source) for source, target in forward]
        low = lax.ppermute(
            lax.slice_in_dim(block, block.shape[dim] - width, None, axis=dim), axis, forward
        )
        high = lax.ppermute(lax.slice_in_dim(block, 0, width, axis=dim), axis, backward)
        block = jnp.concatenate([low, block, high], axis=dim)
    return block


def lookup(table, region):
    total = jnp.zeros(table.shape[:-1] + region.shape, jnp.float32)
    for which in range(table.shape[-1]):
        total = total + table[..., which, None, None] * (region == which).astype(jnp.float32)
    return total


def laplace_padded(padded):
    center = padded[..., 1:-1, :]
    zeros = jnp.zeros(center.shape[:-1] + (1,), jnp.float32)
    right = jnp.concatenate([center[..., 1:], zeros], -1)
    left = jnp.concatenate([zeros, center[..., :-1]], -1)
    return 4.0 * center - padded[..., 2:, :] - padded[..., :-2, :] - right - left


def body(rhs, initial, region, base_table, term_table, galerkin, block_mask, block_inverse):
    terms = galerkin.shape[0]
    modes_all = galerkin.shape[1]
    blocks = block_mask.shape[1]
    width = modes_all // blocks
    shaped = galerkin.reshape(terms, blocks, width, blocks, width)
    coupling = (shaped * block_mask[:, :, None, :, None].astype(jnp.bfloat16)).reshape(
        terms, modes_all, modes_all
    )
    base = lookup(base_table, region)
    coef = lookup(term_table, region)
    rhs_float = rhs.astype(jnp.float32)
    inverse_base = 1.0 / (4.0 * base[:, None])
    u_field = initial.astype(jnp.float32)
    for sweep in range(SWEEPS):
        padded = with_halo(u_field, (("space", 2),), 1)
        local = base[:, None] * laplace_padded(padded)
        rounded = lax.optimization_barrier(padded.astype(jnp.bfloat16)).astype(jnp.float32)
        lap_rounded = laplace_padded(rounded)
        tiles = (coef[:, :, None] * lap_rounded[:, None]).astype(jnp.bfloat16)
        mix_tiles = lax.all_to_all(tiles, "modes", split_axis=3, concat_axis=2, tiled=True)
        coupled = lax.all_to_all(
            jnp.einsum(
                "kij,fkjxy->fixy", coupling, mix_tiles, preferred_element_type=jnp.float32
            ).astype(jnp.bfloat16),
            "modes",
            split_axis=1,
            concat_axis=2,
            tiled=True,
        )
        resid = rhs_float - local - coupled.astype(jnp.float32)
        scaled = resid * inverse_base
        fields, modes_dev, cells_x, cells_y = scaled.shape
        grouped = scaled.reshape(fields, modes_dev // width, width, cells_x, cells_y)
        update = jnp.einsum(
            "bac,fbcxy->fbaxy", block_inverse, grouped, precision=lax.Precision.HIGHEST
        )
        u_field = u_field + 0.6 * update.reshape(fields, modes_dev, cells_x, cells_y)
    return u_field


def solution(mesh):
    in_specs = (
        P(None, "modes", "space", None),
        P(None, "modes", "space", None),
        P("space", None),
        P(),
        P(),
        P(),
        P(),
        P("modes", None, None),
    )
    out_specs = P(None, "modes", "space", None)
    return jax.shard_map(body, mesh=mesh, in_specs=in_specs, out_specs=out_specs, check_vma=False)
```

profile of v0, /device:TPU:16, one launch (start us, length us, event | category | flops | bytes accessed | tf_op | source)
XLA Modules:
  0.0 182.6 jit_solution(13610392275170002387)
XLA Ops:
  0.0 1.4 fusion.72
  1.5 1.9 %collective-permute-start.1 = (f32[2,16,1,512]{3,1,2,0:T(8,128)S(1)}, f32[2,16,1,512]{3,1,2,0:T(8,128)S(1)}, u32[]{:S(2)}, u32[]{:S(2)}) collective-permute-start(f32[2,16,1,512]{3,1,2,0:T(8,128)S(1)} %get-tuple-element.22), channel_id=1, source_target_pairs={{0,16},{16,32},{32,48},{48,64},{64,80},{80,96},{96,112},{112,128},... | collective-permute-start | bytes 196616 | tf_op jit(solution)/shard_map/ppermute | solution.py:15
  3.4 4.5 %collective-permute-start = (f32[2,16,1,512]{3,1,2,0:T(8,128)S(1)}, f32[2,16,1,512]{3,1,2,0:T(8,128)S(1)}, u32[]{:S(2)}, u32[]{:S(2)}) collective-permute-start(f32[2,16,1,512]{3,1,2,0:T(8,128)S(1)} %get-tuple-element.21), channel_id=1, source_target_pairs={{16,0},{32,16},{48,32},{64,48},{80,64},{96,80},{112,96},{128,112},... | collective-permute-start | bytes 196616 | tf_op jit(solution)/shard_map/ppermute | solution.py:18
  8.1 0.1 copy.73
  8.3 0.1 copy.75
  8.4 0.1 copy.76
  8.5 0.1 copy.77
  8.6 0.1 copy.78
  8.7 0.1 copy.79
  8.8 0.1 copy.80
  8.9 0.4 multiply_add_fusion
  9.3 0.5 collective-permute-done
  9.9 0.4 fusion.71
  10.4 0.1 convert_element_type.108
  10.6 1.6 multiply_convert_fusion.1
  12.2 13.0 %all-to-all-start = ((bf16[2,3,16,16,512]{4,2,1,0,3:T(8,128)(2,1)}), bf16[2,3,16,16,512]{4,2,1,0,3:T(8,128)(2,1)S(1)}, u32[]{:S(2)}, u32[]{:S(2)}) async-start(bf16[2,3,16,16,512]{4,2,1,0,3:T(8,128)(2,1)} %multiply_convert_fusion.1), calls=%async_computation | async-start | bytes 3145728 | tf_op jit(solution)/shard_map/all_to_all | solution.py:58
  25.3 2.1 %mul.509 = bf16[3,16,16,16,16]{4,3,2,1,0:T(8,128)(2,1)} broadcast(bf16[3,16,16]{2,1,0:T(8,128)(2,1)S(1)} %convert_element_type.110), dimensions={0,1,3} | broadcast | bytes 394752 | tf_op jit(solution)/shard_map/mul | solution.py:44
  27.4 4.4 %mul.510 = bf16[3,256,256]{2,1,0:T(8,128)(2,1)S(1)} reshape(bf16[3,16,16,16,16]{4,3,2,1,0:T(8,128)(2,1)} %mul.509) | data formatting | bytes 786432 | tf_op jit(solution)/shard_map/mul | solution.py:44
  31.8 34.9 %all-to-all-done = bf16[2,3,16,16,512]{4,2,1,0,3:T(8,128)(2,1)S(1)} async-done(((bf16[2,3,16,16,512]{4,2,1,0,3:T(8,128)(2,1)}), bf16[2,3,16,16,512]{4,2,1,0,3:T(8,128)(2,1)S(1)}, u32[]{:S(2)}, u32[]{:S(2)}) %all-to-all-start) | async-done | bytes 1572896 | tf_op jit(solution)/shard_map/all_to_all | solution.py:58
  66.7 0.1 copy.83
  66.9 0.9 copy-done.21
  67.7 0.6 fusion.7
  68.4 1.2 copy.85
  69.6 3.6 %all-to-all-start.1 = ((bf16[2,256,1,512]{3,0,2,1:T(2,128)(2,1)}), bf16[2,256,1,512]{3,0,2,1:T(2,128)(2,1)S(1)}, u32[]{:S(2)}, u32[]{:S(2)}) async-start(bf16[2,256,1,512]{3,0,2,1:T(2,128)(2,1)} %copy.85), calls=%async_computation.1 | async-start | bytes 1048576 | tf_op jit(solution)/shard_map/all_to_all | solution.py:59
  73.2 0.3 slice_reduce_fusion.7
  73.5 0.1 multiply_divide_fusion
  73.6 1.4 fusion.68
  75.0 17.1 %all-to-all-done.1 = bf16[2,256,1,512]{3,0,2,1:T(2,128)(2,1)S(1)} async-done(((bf16[2,256,1,512]{3,0,2,1:T(2,128)(2,1)}), bf16[2,256,1,512]{3,0,2,1:T(2,128)(2,1)S(1)}, u32[]{:S(2)}, u32[]{:S(2)}) %all-to-all-start.1) | async-done | bytes 524320 | tf_op jit(solution)/shard_map/all_to_all | solution.py:59
  92.1 3.3 %fusion.74 = (bf16[2,16,16,512]{3,1,2,0:T(8,128)(2,1)S(1)}, f32[2,16,16,512]{3,1,2,0:T(8,128)S(1)}) fusion(f32[2,16,16,512]{3,1,2,0:T(8,128)S(1)} %get-tuple-element.28, f32[1,16,16]{2,1,0:T(8,128)S(1)} %copy-done, f32[2,16,1,512]{3,1,2,0:T(8,128)} %copy-done.11, f32[2,16,1,512]{3,1,2,0:T(8,128)} %copy-done.12, ...), kind=kOutput, calls=%fused_computation.108 | convolution fusion | flops 54525952 | bytes 6026240 | tf_op jit(solution)/shard_map/bac,fbcxy->fbaxy/dot_general | solution.py:72
  95.5 1.9 %collective-permute-start.3 = (f32[2,16,1,512]{3,1,2,0:T(8,128)S(1)}, f32[2,16,1,512]{3,1,2,0:T(8,128)S(1)}, u32[]{:S(2)}, u32[]{:S(2)}) collective-permute-start(f32[2,16,1,512]{3,1,2,0:T(8,128)S(1)} %get-tuple-element.18), channel_id=1, source_target_pairs={{0,16},{16,32},{32,48},{48,64},{64,80},{80,96},{96,112},{112,128},... | collective-permute-start | bytes 196616 | tf_op jit(solution)/shard_map/ppermute | solution.py:15
  97.4 4.5 %collective-permute-start.2 = (f32[2,16,1,512]{3,1,2,0:T(8,128)S(1)}, f32[2,16,1,512]{3,1,2,0:T(8,128)S(1)}, u32[]{:S(2)}, u32[]{:S(2)}) collective-permute-start(f32[2,16,1,512]{3,1,2,0:T(8,128)S(1)} %get-tuple-element.17), channel_id=1, source_target_pairs={{16,0},{32,16},{48,32},{64,48},{80,64},{96,80},{112,96},{128,112},... | collective-permute-start | bytes 196616 | tf_op jit(solution)/shard_map/ppermute | solution.py:18
  102.0 1.8 %collective-permute-done.2 = f32[2,16,1,512]{3,1,2,0:T(8,128)S(1)} collective-permute-done((f32[2,16,1,512]{3,1,2,0:T(8,128)S(1)}, f32[2,16,1,512]{3,1,2,0:T(8,128)S(1)}, u32[]{:S(2)}, u32[]{:S(2)}) %collective-permute-start.2) | collective-permute-done | bytes 65568 | tf_op jit(solution)/shard_map/ppermute | solution.py:18
  103.9 0.6 copy-done.15
  104.5 0.4 fusion.70
  104.9 0.1 convert_element_type.118
  105.1 0.5 multiply_convert_fusion
  105.6 45.6 %all_to_all.48 = bf16[2,3,16,16,512]{4,2,1,0,3:T(8,128)(2,1)S(1)} all-to-all(bf16[2,3,16,16,512]{4,2,1,0,3:T(8,128)(2,1)S(1)} %multiply_convert_fusion), channel_id=1, replica_groups=mesh['space'=32,'modes'=16] {'modes'}, dimensions={3} | all-to-all | bytes 3145728 | tf_op jit(solution)/shard_map/all_to_all | solution.py:58
  151.1 0.2 copy.88
  151.3 0.8 copy-done.2
  152.1 0.1 copy-done.22
  152.2 0.7 fusion.6
  152.9 1.2 copy.90
  154.1 4.4 %all-to-all-start.3 = ((bf16[2,256,1,512]{3,0,2,1:T(2,128)(2,1)}), bf16[2,256,1,512]{3,0,2,1:T(2,128)(2,1)}, u32[]{:S(2)}, u32[]{:S(2)}) async-start(bf16[2,256,1,512]{3,0,2,1:T(2,128)(2,1)} %copy.90), calls=%async_computation.3 | async-start | bytes 1048576 | tf_op jit(solution)/shard_map/all_to_all | solution.py:59
  158.5 0.4 fusion.66
  158.9 18.0 %all-to-all-done.3 = bf16[2,256,1,512]{3,0,2,1:T(2,128)(2,1)} async-done(((bf16[2,256,1,512]{3,0,2,1:T(2,128)(2,1)}), bf16[2,256,1,512]{3,0,2,1:T(2,128)(2,1)}, u32[]{:S(2)}, u32[]{:S(2)}) %all-to-all-start.3) | async-done | bytes 524320 | tf_op jit(solution)/shard_map/all_to_all | solution.py:59
  176.9 1.1 copy.91
  178.0 2.9 %fusion.1 = f32[2,16,16,512]{3,1,2,0:T(8,128)S(1)} fusion(f32[2,16,16,512]{3,1,2,0:T(8,128)S(1)} %get-tuple-element.46, f32[2,16,1,512]{3,1,2,0:T(8,128)S(1)} %copy-done.14, f32[2,16,1,512]{3,1,2,0:T(8,128)S(1)} %copy-done.16, bf16[2,16,16,1,512]{4,2,1,0,3:T(8,128)(2,1)S(1)} %bitcast.97, f32[2,16,16,511]{3,1,2,0:T(8,128)S(1)} %get-tuple-element.16, ...), kind=kOutput, calls=%fused_computation.4 | convolution fusion | flops 54263808 | bytes 5501952 | tf_op jit(solution)/shard_map/bac,fbcxy->fbaxy/dot_general | solution.py:72
  181.0 1.6 copy.92
  (57 shorter events, 0.6 us)
Async XLA Ops:
  0.0 92.1 %copy-start = (f32[1,16,16]{2,1,0:T(8,128)S(1)}, f32[1,16,16]{2,1,0:T(8,128)}, u32[]{:S(2)}) copy-start(f32[1,16,16]{2,1,0:T(8,128)} %param.15) | copy-start | bytes 3076
  0.0 7.9 %copy-start.19 = (s32[16,512]{1,0:T(8,128)S(1)}, s32[16,512]{1,0:T(8,128)}, u32[]{:S(2)}) copy-start(s32[16,512]{1,0:T(8,128)} %param.10) | copy-start | bytes 98308
  0.0 8.0 %copy-start.17 = (f32[2,3,8]{2,0,1:T(2,128)S(1)}, f32[2,3,8]{2,0,1:T(2,128)}, u32[]{:S(2)}) copy-start(f32[2,3,8]{2,0,1:T(2,128)} %param.12) | copy-start | bytes 580
  1.5 7.8 %collective-permute-start.1 = (f32[2,16,1,512]{3,1,2,0:T(8,128)S(1)}, f32[2,16,1,512]{3,1,2,0:T(8,128)S(1)}, u32[]{:S(2)}, u32[]{:S(2)}) collective-permute-start(f32[2,16,1,512]{3,1,2,0:T(8,128)S(1)} %get-tuple-element.22), channel_id=1, source_target_pairs={{0,16},{16,32},{32,48},{48,64},{64,80},{80,96},{96,112},{112,128},... | collective-permute-start | bytes 196616 | tf_op jit(solution)/shard_map/ppermute | solution.py:15
  3.4 6.4 %collective-permute-start = (f32[2,16,1,512]{3,1,2,0:T(8,128)S(1)}, f32[2,16,1,512]{3,1,2,0:T(8,128)S(1)}, u32[]{:S(2)}, u32[]{:S(2)}) collective-permute-start(f32[2,16,1,512]{3,1,2,0:T(8,128)S(1)} %get-tuple-element.21), channel_id=1, source_target_pairs={{16,0},{32,16},{48,32},{64,48},{80,64},{96,80},{112,96},{128,112},... | collective-permute-start | bytes 196616 | tf_op jit(solution)/shard_map/ppermute | solution.py:18
  8.0 2.3 %copy-start.3 = (f32[16,512]{1,0:T(8,128)}, f32[16,512]{1,0:T(8,128)S(1)}, u32[]{:S(2)}) copy-start(f32[16,512]{1,0:T(8,128)S(1)} %get-tuple-element.33) | copy-start | bytes 98308
  8.0 2.3 %copy-start.5 = (f32[16,512]{1,0:T(8,128)}, f32[16,512]{1,0:T(8,128)S(1)}, u32[]{:S(2)}) copy-start(f32[16,512]{1,0:T(8,128)S(1)} %get-tuple-element.34) | copy-start | bytes 98308
  8.0 2.3 %copy-start.7 = (f32[16,512]{1,0:T(8,128)}, f32[16,512]{1,0:T(8,128)S(1)}, u32[]{:S(2)}) copy-start(f32[16,512]{1,0:T(8,128)S(1)} %get-tuple-element.35) | copy-start | bytes 98308
  8.0 2.3 %copy-start.9 = (f32[16,512]{1,0:T(8,128)}, f32[16,512]{1,0:T(8,128)S(1)}, u32[]{:S(2)}) copy-start(f32[16,512]{1,0:T(8,128)S(1)} %get-tuple-element.36) | copy-start | bytes 98308
  9.3 1.1 copy-start.11
  9.8 0.6 copy-start.12
  12.2 13.0 %copy-start.20 = (s32[3,16,16]{2,1,0:T(8,128)S(1)}, s32[3,16,16]{2,1,0:T(8,128)}, u32[]{:S(2)}) copy-start(s32[3,16,16]{2,1,0:T(8,128)} %param.14) | copy-start | bytes 9220
  12.2 54.5 %all-to-all-start = ((bf16[2,3,16,16,512]{4,2,1,0,3:T(8,128)(2,1)}), bf16[2,3,16,16,512]{4,2,1,0,3:T(8,128)(2,1)S(1)}, u32[]{:S(2)}, u32[]{:S(2)}) async-start(bf16[2,3,16,16,512]{4,2,1,0,3:T(8,128)(2,1)} %multiply_convert_fusion.1), calls=%async_computation | async-start | bytes 3145728 | tf_op jit(solution)/shard_map/all_to_all | solution.py:58
  31.8 35.1 %copy-start.1 = (bf16[3,256,256]{2,1,0:T(8,128)(2,1)}, bf16[3,256,256]{2,1,0:T(8,128)(2,1)S(1)}, u32[]{:S(2)}) copy-start(bf16[3,256,256]{2,1,0:T(8,128)(2,1)S(1)} %mul.510) | copy-start | bytes 1179652
  66.7 1.0 copy-start.21
  68.4 4.8 %copy-start.18 = (f32[2,8]{1,0:T(2,128)S(1)}, f32[2,8]{1,0:T(2,128)}, u32[]{:S(2)}) copy-start(f32[2,8]{1,0:T(2,128)} %param.11) | copy-start | bytes 196
  68.4 5.1 %copy-start.4 = (f32[16,512]{1,0:T(8,128)S(1)}, f32[16,512]{1,0:T(8,128)}, u32[]{:S(2)}) copy-start(f32[16,512]{1,0:T(8,128)} %copy-done.3) | copy-start | bytes 98308
  68.4 5.1 %copy-start.6 = (f32[16,512]{1,0:T(8,128)S(1)}, f32[16,512]{1,0:T(8,128)}, u32[]{:S(2)}) copy-start(f32[16,512]{1,0:T(8,128)} %copy-done.5) | copy-start | bytes 98308
  68.4 5.1 %copy-start.8 = (f32[16,512]{1,0:T(8,128)S(1)}, f32[16,512]{1,0:T(8,128)}, u32[]{:S(2)}) copy-start(f32[16,512]{1,0:T(8,128)} %copy-done.7) | copy-start | bytes 98308
  68.4 5.1 %copy-start.10 = (f32[16,512]{1,0:T(8,128)S(1)}, f32[16,512]{1,0:T(8,128)}, u32[]{:S(2)}) copy-start(f32[16,512]{1,0:T(8,128)} %copy-done.9) | copy-start | bytes 98308
  69.6 22.5 %all-to-all-start.1 = ((bf16[2,256,1,512]{3,0,2,1:T(2,128)(2,1)}), bf16[2,256,1,512]{3,0,2,1:T(2,128)(2,1)S(1)}, u32[]{:S(2)}, u32[]{:S(2)}) async-start(bf16[2,256,1,512]{3,0,2,1:T(2,128)(2,1)} %copy.85), calls=%async_computation.1 | async-start | bytes 1048576 | tf_op jit(solution)/shard_map/all_to_all | solution.py:59
  95.5 6.5 %collective-permute-start.3 = (f32[2,16,1,512]{3,1,2,0:T(8,128)S(1)}, f32[2,16,1,512]{3,1,2,0:T(8,128)S(1)}, u32[]{:S(2)}, u32[]{:S(2)}) collective-permute-start(f32[2,16,1,512]{3,1,2,0:T(8,128)S(1)} %get-tuple-element.18), channel_id=1, source_target_pairs={{0,16},{16,32},{32,48},{48,64},{64,80},{80,96},{96,112},{112,128},... | collective-permute-start | bytes 196616 | tf_op jit(solution)/shard_map/ppermute | solution.py:15
  97.4 6.4 %collective-permute-start.2 = (f32[2,16,1,512]{3,1,2,0:T(8,128)S(1)}, f32[2,16,1,512]{3,1,2,0:T(8,128)S(1)}, u32[]{:S(2)}, u32[]{:S(2)}) collective-permute-start(f32[2,16,1,512]{3,1,2,0:T(8,128)S(1)} %get-tuple-element.17), channel_id=1, source_target_pairs={{16,0},{32,16},{48,32},{64,48},{80,64},{96,80},{112,96},{128,112},... | collective-permute-start | bytes 196616 | tf_op jit(solution)/shard_map/ppermute | solution.py:18
  102.0 1.9 %copy-start.13 = (f32[2,16,1,512]{3,1,2,0:T(8,128)}, f32[2,16,1,512]{3,1,2,0:T(8,128)S(1)}, u32[]{:S(2)}) copy-start(f32[2,16,1,512]{3,1,2,0:T(8,128)S(1)} %collective-permute-done.3) | copy-start | bytes 196612
  103.9 0.6 copy-start.15
  151.1 1.0 copy-start.2
  151.1 1.1 copy-start.22
  154.1 22.8 %all-to-all-start.3 = ((bf16[2,256,1,512]{3,0,2,1:T(2,128)(2,1)}), bf16[2,256,1,512]{3,0,2,1:T(2,128)(2,1)}, u32[]{:S(2)}, u32[]{:S(2)}) async-start(bf16[2,256,1,512]{3,0,2,1:T(2,128)(2,1)} %copy.90), calls=%async_computation.3 | async-start | bytes 1048576 | tf_op jit(solution)/shard_map/all_to_all | solution.py:59
  158.5 19.5 %copy-start.14 = (f32[2,16,1,512]{3,1,2,0:T(8,128)S(1)}, f32[2,16,1,512]{3,1,2,0:T(8,128)}, u32[]{:S(2)}) copy-start(f32[2,16,1,512]{3,1,2,0:T(8,128)} %copy-done.13) | copy-start | bytes 196612
  158.5 19.5 %copy-start.16 = (f32[2,16,1,512]{3,1,2,0:T(8,128)S(1)}, f32[2,16,1,512]{3,1,2,0:T(8,128)}, u32[]{:S(2)}) copy-start(f32[2,16,1,512]{3,1,2,0:T(8,128)} %copy-done.15) | copy-start | bytes 196612
where the time goes:
time: 183 us
  waiting for transfers between devices  72.4 us (40%)
  blocking collectives  45.6 us (25%)
  starting transfers between devices  33.9 us (19%)
  local copies, waits for them, and re-layouts  18.1 us (10%)
  matrix products  7.59 us (4%)
  other arithmetic  4.48 us (2%)
    all_to_all x1, blocking collectives, body(): lax.all_to_all(tiles, 'modes', split_axis=3, concat_axis=2, tiled=True)  45.6 us
    all_to_all x2, waiting for transfers between devices, body(): lax.all_to_all(jnp.einsum('kij,fkjxy->fixy', coupling, mix_tiles, preferr...  35.1 us
    all_to_all x1, waiting for transfers between devices, body(): lax.all_to_all(tiles, 'modes', split_axis=3, concat_axis=2, tiled=True)  34.9 us
    all_to_all x1, starting transfers between devices, body(): lax.all_to_all(tiles, 'modes', split_axis=3, concat_axis=2, tiled=True)  13 us
    ppermute x2, starting transfers between devices, with_halo(): lax.ppermute(lax.slice_in_dim(block, 0, width, axis=dim), axis, backward)  9.08 us
    all_to_all x2, starting transfers between devices, body(): lax.all_to_all(jnp.einsum('kij,fkjxy->fixy', coupling, mix_tiles, preferr...  7.99 us
    mul x2, local copies, waits for them, and re-layouts, body(): shaped * block_mask[:, :, None, :, None].astype(jnp.bfloat16)  6.52 us
    dot_general x2, matrix products, body(): jnp.einsum('bac,fbcxy->fbaxy', block_inverse, grouped, precision=lax.Prec...  6.29 us
  transfers between devices with their start and end apart: 7, of which 5 were waited for; matrix products, arithmetic and copies ran while one was open for 5% of the time, Pallas kernels for 0%

commit v1 on v0

--- a/solution.py
+++ b/solution.py
@@ -56,14 +56,25 @@
         lap_rounded = laplace_padded(rounded)
         tiles = (coef[:, :, None] * lap_rounded[:, None]).astype(jnp.bfloat16)
         mix_tiles = lax.all_to_all(tiles, "modes", split_axis=3, concat_axis=2, tiled=True)
-        coupled = lax.all_to_all(
-            jnp.einsum(
-                "kij,fkjxy->fixy", coupling, mix_tiles, preferred_element_type=jnp.float32
-            ).astype(jnp.bfloat16),
-            "modes",
-            split_axis=1,
-            concat_axis=2,
-            tiled=True,
+        coupled = jnp.concatenate(
+            lax.all_to_all(
+                jnp.stack(
+                    jnp.split(
+                        jnp.einsum(
+                            "kij,fkjxy->fixy",
+                            coupling,
+                            mix_tiles,
+                            preferred_element_type=jnp.float32,
+                        ).astype(jnp.bfloat16),
+                        lax.axis_size("modes"),
+                        axis=1,
+                    )
+                ),
+                "modes",
+                0,
+                0,
+            ),
+            axis=2,
         )
         resid = rhs_float - local - coupled.astype(jnp.float32)
         scaled = resid * inverse_base

time: 183 us -> 202 us (1.10)
  local copies, waits for them, and re-layouts: 18.1 us -> 36.8 us
    unnamed x46 -> x82, local copies, waits for them, and re-layouts: 2.55 us -> 22.2 us
    convert_element_type x2 -> x0, local copies, waits for them, and re-layouts: 2.34 us -> none  [body(): coupled = lax.all_to_all(jnp.einsum('kij,fkjxy->fixy', coupling, mix_tile...]
  transfers between devices with their start and end apart: 7 -> 7, of which waited for: 5 -> 5; matrix products, arithmetic and copies ran while one was open for 5% -> 6% of each run, Pallas kernels for 0% -> 0%
where the time goes in v1:
time: 202 us; the launch traced here: 201 us
  waiting for transfers between devices  71 us (35%)
  blocking collectives  45.6 us (23%)
  local copies, waits for them, and re-layouts  36.8 us (18%)
  starting transfers between devices  33.9 us (17%)
  matrix products  7.73 us (4%)
  other arithmetic  5.6 us (3%)
    all_to_all x1, blocking collectives, body(): lax.all_to_all(tiles, 'modes', split_axis=3, concat_axis=2, tiled=True)  45.6 us
    all_to_all x1, waiting for transfers between devices, body(): lax.all_to_all(tiles, 'modes', split_axis=3, concat_axis=2, tiled=True)  35 us
    all_to_all x2, waiting for transfers between devices, body(): lax.all_to_all(jnp.stack(jnp.split(jnp.einsum('kij,fkjxy->fixy', coupling...  33.7 us
    unnamed x82, local copies, waits for them, and re-layouts  22.2 us
    all_to_all x1, starting transfers between devices, body(): lax.all_to_all(tiles, 'modes', split_axis=3, concat_axis=2, tiled=True)  13 us
    ppermute x2, starting transfers between devices, with_halo(): lax.ppermute(lax.slice_in_dim(block, 0, width, axis=dim), axis, backward)  9.08 us
    all_to_all x2, starting transfers between devices, body(): lax.all_to_all(jnp.stack(jnp.split(jnp.einsum('kij,fkjxy->fixy', coupling...  8.01 us
    dot_general x2, matrix products, body(): jnp.einsum('bac,fbcxy->fbaxy', block_inverse, grouped, precision=lax.Prec...  6.56 us
  transfers between devices with their start and end apart: 7, of which 5 were waited for; matrix products, arithmetic and copies ran while one was open for 6% of the time, Pallas kernels for 0%

profile of v1, /device:TPU:16, one launch (start us, length us, event | category | flops | bytes accessed | tf_op | source)
XLA Modules:
  0.0 201.3 jit_solution(17966568761862463102)
XLA Ops:
  0.0 1.4 fusion.73
  1.5 1.9 collective-permute-start.1
  3.4 4.5 %collective-permute-start = (f32[2,16,1,512]{3,1,0,2:T(8,128)S(1)}, f32[2,16,1,512]{3,1,0,2:T(8,128)S(1)}, u32[]{:S(2)}, u32[]{:S(2)}) collective-permute-start(f32[2,16,1,512]{3,1,0,2:T(8,128)S(1)} %get-tuple-element.21), channel_id=1, source_target_pairs={{16,0},{32,16},{48,32},{64,48},{80,64},{96,80},{112,96},{128,112},... | collective-permute-start | bytes 196616 | tf_op jit(solution)/shard_map/ppermute | solution.py:18
  11.1 1.7 multiply_convert_fusion.1
  12.8 13.0 %all-to-all-start = ((bf16[2,3,16,16,512]{4,2,1,0,3:T(8,128)(2,1)}), bf16[2,3,16,16,512]{4,2,1,0,3:T(8,128)(2,1)S(1)}, u32[]{:S(2)}, u32[]{:S(2)}) async-start(bf16[2,3,16,16,512]{4,2,1,0,3:T(8,128)(2,1)} %multiply_convert_fusion.1), calls=%async_computation | async-start | bytes 3145728 | tf_op jit(solution)/shard_map/all_to_all | solution.py:58
  25.8 2.1 %mul.509 = bf16[3,16,16,16,16]{4,3,2,1,0:T(8,128)(2,1)} broadcast(bf16[3,16,16]{2,1,0:T(8,128)(2,1)S(1)} %convert_element_type.104), dimensions={0,1,3} | broadcast | bytes 394752 | tf_op jit(solution)/shard_map/mul | solution.py:44
  27.9 4.4 %mul.510 = bf16[3,256,256]{2,1,0:T(8,128)(2,1)S(1)} reshape(bf16[3,16,16,16,16]{4,3,2,1,0:T(8,128)(2,1)} %mul.509) | data formatting | bytes 786432 | tf_op jit(solution)/shard_map/mul | solution.py:44
  32.4 35.0 %all-to-all-done = bf16[2,3,16,16,512]{4,2,1,0,3:T(8,128)(2,1)S(1)} async-done(((bf16[2,3,16,16,512]{4,2,1,0,3:T(8,128)(2,1)}), bf16[2,3,16,16,512]{4,2,1,0,3:T(8,128)(2,1)S(1)}, u32[]{:S(2)}, u32[]{:S(2)}) %all-to-all-start) | async-done | bytes 1572896 | tf_op jit(solution)/shard_map/all_to_all | solution.py:58
  67.4 0.9 copy-done.4
  69.0 0.6 constant_dynamic-update-slice_fusion.15
  69.6 0.6 constant_dynamic-update-slice_fusion.14
  71.4 0.6 constant_dynamic-update-slice_fusion.11
  72.0 0.6 constant_dynamic-update-slice_fusion.10
  72.6 0.6 constant_dynamic-update-slice_fusion.9
  73.3 0.6 constant_dynamic-update-slice_fusion.8
  75.1 0.6 constant_dynamic-update-slice_fusion.5
  78.8 3.6 %all-to-all-start.1 = ((bf16[16,2,16,1,512]{4,2,1,3,0:T(8,128)(2,1)}), bf16[16,2,16,1,512]{4,2,1,3,0:T(8,128)(2,1)S(1)}, u32[]{:S(2)}, u32[]{:S(2)}) async-start(bf16[16,2,16,1,512]{4,2,1,3,0:T(8,128)(2,1)} %constant_dynamic-update-slice_fusion), calls=%async_computation.1 | async-start | bytes 1048576 | tf_op jit(solution)/shard_map/all_to_all | solution.py:60
  82.8 0.7 copy.63
  83.5 0.7 copy.74
  84.2 1.4 fusion.69
  85.5 15.7 %all-to-all-done.1 = bf16[16,2,16,1,512]{4,2,1,3,0:T(8,128)(2,1)S(1)} async-done(((bf16[16,2,16,1,512]{4,2,1,3,0:T(8,128)(2,1)}), bf16[16,2,16,1,512]{4,2,1,3,0:T(8,128)(2,1)S(1)}, u32[]{:S(2)}, u32[]{:S(2)}) %all-to-all-start.1) | async-done | bytes 524320 | tf_op jit(solution)/shard_map/all_to_all | solution.py:60
  101.2 0.8 copy-done.3
  102.0 3.5 %fusion.75 = (bf16[2,16,16,512]{3,1,0,2:T(8,128)(2,1)S(1)}, f32[2,16,16,512]{3,1,0,2:T(8,128)S(1)}) fusion(f32[2,16,16,512]{3,1,0,2:T(8,128)S(1)} %get-tuple-element.28, f32[1,16,16]{2,1,0:T(8,128)S(1)} %copy-done, f32[2,16,1,512]{3,1,0,2:T(8,128)} %copy-done.16, f32[2,16,1,512]{3,1,0,2:T(8,128)} %copy-done.17, bf16[16,2,16,1,512]{4,2,1,3,0:T(8,128)(2,1)} %copy-done.3, ...), kind=kOutput, calls=%fused_computation.173 | convolution fusion | flops 54525952 | bytes 6026240 | tf_op jit(solution)/shard_map/bac,fbcxy->fbaxy/dot_general | solution.py:83
  105.6 1.9 collective-permute-start.3
  107.5 4.5 %collective-permute-start.2 = (f32[2,16,1,512]{3,1,0,2:T(8,128)S(1)}, f32[2,16,1,512]{3,1,0,2:T(8,128)S(1)}, u32[]{:S(2)}, u32[]{:S(2)}) collective-permute-start(f32[2,16,1,512]{3,1,0,2:T(8,128)S(1)} %get-tuple-element.17), channel_id=1, source_target_pairs={{16,0},{32,16},{48,32},{64,48},{80,64},{96,80},{112,96},{128,112},... | collective-permute-start | bytes 196616 | tf_op jit(solution)/shard_map/ppermute | solution.py:18
  112.1 1.8 collective-permute-done.2
  116.7 45.6 %all_to_all.40 = bf16[2,3,16,16,512]{4,2,1,0,3:T(8,128)(2,1)S(1)} all-to-all(bf16[2,3,16,16,512]{4,2,1,0,3:T(8,128)(2,1)S(1)} %multiply_convert_fusion), channel_id=1, replica_groups=mesh['space'=32,'modes'=16] {'modes'}, dimensions={3} | all-to-all | bytes 3145728 | tf_op jit(solution)/shard_map/all_to_all | solution.py:58
  162.4 0.8 copy-done.5
  163.9 0.6 constant_dynamic-update-slice_fusion.31
  164.5 0.6 constant_dynamic-update-slice_fusion.30
  165.1 0.6 constant_dynamic-update-slice_fusion.29
  165.7 0.6 constant_dynamic-update-slice_fusion.28
  166.3 0.6 constant_dynamic-update-slice_fusion.27
  167.0 0.6 constant_dynamic-update-slice_fusion.26
  167.6 0.6 constant_dynamic-update-slice_fusion.25
  168.2 0.6 constant_dynamic-update-slice_fusion.24
  168.8 0.6 constant_dynamic-update-slice_fusion.23
  169.4 0.6 constant_dynamic-update-slice_fusion.22
  170.0 0.6 constant_dynamic-update-slice_fusion.21
  170.7 0.6 constant_dynamic-update-slice_fusion.20
  171.3 0.6 constant_dynamic-update-slice_fusion.19
  171.9 0.6 constant_dynamic-update-slice_fusion.18
  172.5 0.6 constant_dynamic-update-slice_fusion.17
  173.1 0.6 constant_dynamic-update-slice_fusion.16
  173.7 4.4 %all-to-all-start.3 = ((bf16[16,2,16,1,512]{4,2,1,3,0:T(8,128)(2,1)}), bf16[16,2,16,1,512]{4,2,1,3,0:T(8,128)(2,1)}, u32[]{:S(2)}, u32[]{:S(2)}) async-start(bf16[16,2,16,1,512]{4,2,1,3,0:T(8,128)(2,1)} %constant_dynamic-update-slice_fusion.16), calls=%async_computation.3 | async-start | bytes 1048576 | tf_op jit(solution)/shard_map/all_to_all | solution.py:60
  178.6 18.0 %all-to-all-done.3 = bf16[16,2,16,1,512]{4,2,1,3,0:T(8,128)(2,1)} async-done(((bf16[16,2,16,1,512]{4,2,1,3,0:T(8,128)(2,1)}), bf16[16,2,16,1,512]{4,2,1,3,0:T(8,128)(2,1)}, u32[]{:S(2)}, u32[]{:S(2)}) %all-to-all-start.3) | async-done | bytes 524320 | tf_op jit(solution)/shard_map/all_to_all | solution.py:60
  196.6 3.1 %fusion.1 = f32[2,16,16,512]{3,1,0,2:T(8,128)S(1)} fusion(f32[2,16,16,512]{3,1,0,2:T(8,128)S(1)} %get-tuple-element.46, f32[2,16,1,512]{3,1,0,2:T(8,128)S(1)} %copy-done.19, f32[2,16,1,512]{3,1,0,2:T(8,128)S(1)} %copy-done.21, f32[2,16,16,511]{3,1,0,2:T(8,128)S(1)} %get-tuple-element.16, f32[2,16,16,511]{3,1,0,2:T(8,128)S(1)} %get-tuple-element.15, ...), kind=kOutput, calls=%fused_computation.6 | convolution fusion | flops 54263808 | bytes 5501952 | tf_op jit(solution)/shard_map/bac,fbcxy->fbaxy/dot_general | solution.py:83
  199.7 1.6 copy.81
  (95 shorter events, 13.5 us)
Async XLA Ops:
  0.0 102.0 %copy-start = (f32[1,16,16]{2,1,0:T(8,128)S(1)}, f32[1,16,16]{2,1,0:T(8,128)}, u32[]{:S(2)}) copy-start(f32[1,16,16]{2,1,0:T(8,128)} %param.15) | copy-start | bytes 3076
  0.0 7.9 %copy-start.24 = (s32[16,512]{1,0:T(8,128)S(1)}, s32[16,512]{1,0:T(8,128)}, u32[]{:S(2)}) copy-start(s32[16,512]{1,0:T(8,128)} %param.10) | copy-start | bytes 98308
  0.0 8.0 %copy-start.22 = (f32[2,3,8]{2,0,1:T(2,128)S(1)}, f32[2,3,8]{2,0,1:T(2,128)}, u32[]{:S(2)}) copy-start(f32[2,3,8]{2,0,1:T(2,128)} %param.12) | copy-start | bytes 580
  1.5 7.8 %collective-permute-start.1 = (f32[2,16,1,512]{3,1,0,2:T(8,128)S(1)}, f32[2,16,1,512]{3,1,0,2:T(8,128)S(1)}, u32[]{:S(2)}, u32[]{:S(2)}) collective-permute-start(f32[2,16,1,512]{3,1,0,2:T(8,128)S(1)} %get-tuple-element.22), channel_id=1, source_target_pairs={{0,16},{16,32},{32,48},{48,64},{64,80},{80,96},{96,112},{112,128},... | collective-permute-start | bytes 196616 | tf_op jit(solution)/shard_map/ppermute | solution.py:15
  3.4 6.4 %collective-permute-start = (f32[2,16,1,512]{3,1,0,2:T(8,128)S(1)}, f32[2,16,1,512]{3,1,0,2:T(8,128)S(1)}, u32[]{:S(2)}, u32[]{:S(2)}) collective-permute-start(f32[2,16,1,512]{3,1,0,2:T(8,128)S(1)} %get-tuple-element.21), channel_id=1, source_target_pairs={{16,0},{32,16},{48,32},{64,48},{80,64},{96,80},{112,96},{128,112},... | collective-permute-start | bytes 196616 | tf_op jit(solution)/shard_map/ppermute | solution.py:18
  8.0 2.3 %copy-start.8 = (f32[16,512]{1,0:T(8,128)}, f32[16,512]{1,0:T(8,128)S(1)}, u32[]{:S(2)}) copy-start(f32[16,512]{1,0:T(8,128)S(1)} %get-tuple-element.33) | copy-start | bytes 98308
  8.0 2.3 %copy-start.10 = (f32[16,512]{1,0:T(8,128)}, f32[16,512]{1,0:T(8,128)S(1)}, u32[]{:S(2)}) copy-start(f32[16,512]{1,0:T(8,128)S(1)} %get-tuple-element.34) | copy-start | bytes 98308
  8.0 2.3 %copy-start.12 = (f32[16,512]{1,0:T(8,128)}, f32[16,512]{1,0:T(8,128)S(1)}, u32[]{:S(2)}) copy-start(f32[16,512]{1,0:T(8,128)S(1)} %get-tuple-element.35) | copy-start | bytes 98308
  8.0 2.3 %copy-start.14 = (f32[16,512]{1,0:T(8,128)}, f32[16,512]{1,0:T(8,128)S(1)}, u32[]{:S(2)}) copy-start(f32[16,512]{1,0:T(8,128)S(1)} %get-tuple-element.36) | copy-start | bytes 98308
  9.3 1.8 copy-start.1
  9.3 1.1 copy-start.16
  9.8 0.6 copy-start.17
  12.8 13.0 %copy-start.25 = (s32[3,16,16]{2,1,0:T(8,128)S(1)}, s32[3,16,16]{2,1,0:T(8,128)}, u32[]{:S(2)}) copy-start(s32[3,16,16]{2,1,0:T(8,128)} %param.14) | copy-start | bytes 9220
  12.8 54.5 %all-to-all-start = ((bf16[2,3,16,16,512]{4,2,1,0,3:T(8,128)(2,1)}), bf16[2,3,16,16,512]{4,2,1,0,3:T(8,128)(2,1)S(1)}, u32[]{:S(2)}, u32[]{:S(2)}) async-start(bf16[2,3,16,16,512]{4,2,1,0,3:T(8,128)(2,1)} %multiply_convert_fusion.1), calls=%async_computation | async-start | bytes 3145728 | tf_op jit(solution)/shard_map/all_to_all | solution.py:58
  67.3 1.0 copy-start.4
  68.9 13.5 %copy-start.23 = (f32[2,8]{1,0:T(2,128)S(1)}, f32[2,8]{1,0:T(2,128)}, u32[]{:S(2)}) copy-start(f32[2,8]{1,0:T(2,128)} %param.11) | copy-start | bytes 196
  68.9 13.7 %copy-start.9 = (f32[16,512]{1,0:T(8,128)S(1)}, f32[16,512]{1,0:T(8,128)}, u32[]{:S(2)}) copy-start(f32[16,512]{1,0:T(8,128)} %copy-done.8) | copy-start | bytes 98308
  68.9 13.7 %copy-start.11 = (f32[16,512]{1,0:T(8,128)S(1)}, f32[16,512]{1,0:T(8,128)}, u32[]{:S(2)}) copy-start(f32[16,512]{1,0:T(8,128)} %copy-done.10) | copy-start | bytes 98308
  68.9 13.7 %copy-start.13 = (f32[16,512]{1,0:T(8,128)S(1)}, f32[16,512]{1,0:T(8,128)}, u32[]{:S(2)}) copy-start(f32[16,512]{1,0:T(8,128)} %copy-done.12) | copy-start | bytes 98308
  68.9 13.7 %copy-start.15 = (f32[16,512]{1,0:T(8,128)S(1)}, f32[16,512]{1,0:T(8,128)}, u32[]{:S(2)}) copy-start(f32[16,512]{1,0:T(8,128)} %copy-done.14) | copy-start | bytes 98308
  78.8 22.5 %all-to-all-start.1 = ((bf16[16,2,16,1,512]{4,2,1,3,0:T(8,128)(2,1)}), bf16[16,2,16,1,512]{4,2,1,3,0:T(8,128)(2,1)S(1)}, u32[]{:S(2)}, u32[]{:S(2)}) async-start(bf16[16,2,16,1,512]{4,2,1,3,0:T(8,128)(2,1)} %constant_dynamic-update-slice_fusion), calls=%async_computation.1 | async-start | bytes 1048576 | tf_op jit(solution)/shard_map/all_to_all | solution.py:60
  101.2 0.8 copy-start.3
  105.6 6.5 %collective-permute-start.3 = (f32[2,16,1,512]{3,1,0,2:T(8,128)S(1)}, f32[2,16,1,512]{3,1,0,2:T(8,128)S(1)}, u32[]{:S(2)}, u32[]{:S(2)}) collective-permute-start(f32[2,16,1,512]{3,1,0,2:T(8,128)S(1)} %get-tuple-element.18), channel_id=1, source_target_pairs={{0,16},{16,32},{32,48},{48,64},{64,80},{80,96},{96,112},{112,128},... | collective-permute-start | bytes 196616 | tf_op jit(solution)/shard_map/ppermute | solution.py:15
  107.5 6.4 %collective-permute-start.2 = (f32[2,16,1,512]{3,1,0,2:T(8,128)S(1)}, f32[2,16,1,512]{3,1,0,2:T(8,128)S(1)}, u32[]{:S(2)}, u32[]{:S(2)}) collective-permute-start(f32[2,16,1,512]{3,1,0,2:T(8,128)S(1)} %get-tuple-element.17), channel_id=1, source_target_pairs={{16,0},{32,16},{48,32},{64,48},{80,64},{96,80},{112,96},{128,112},... | collective-permute-start | bytes 196616 | tf_op jit(solution)/shard_map/ppermute | solution.py:18
  112.0 1.9 copy-start.18
  113.9 0.6 copy-start.20
  115.2 1.0 copy-start.2
  162.3 1.0 copy-start.5
  173.7 22.8 %all-to-all-start.3 = ((bf16[16,2,16,1,512]{4,2,1,3,0:T(8,128)(2,1)}), bf16[16,2,16,1,512]{4,2,1,3,0:T(8,128)(2,1)}, u32[]{:S(2)}, u32[]{:S(2)}) async-start(bf16[16,2,16,1,512]{4,2,1,3,0:T(8,128)(2,1)} %constant_dynamic-update-slice_fusion.16), calls=%async_computation.3 | async-start | bytes 1048576 | tf_op jit(solution)/shard_map/all_to_all | solution.py:60
  178.2 18.4 %copy-start.6 = (f32[2,16,512]{2,0,1:T(2,128)S(1)}, f32[2,16,512]{2,0,1:T(2,128)}, u32[]{:S(2)}) copy-start(f32[2,16,512]{2,0,1:T(2,128)} %copy.63) | copy-start | bytes 196612
  178.2 18.4 %copy-start.7 = (f32[2,16,512]{2,0,1:T(2,128)S(1)}, f32[2,16,512]{2,0,1:T(2,128)}, u32[]{:S(2)}) copy-start(f32[2,16,512]{2,0,1:T(2,128)} %copy.74) | copy-start | bytes 196612
  178.2 18.4 %copy-start.19 = (f32[2,16,1,512]{3,1,0,2:T(8,128)S(1)}, f32[2,16,1,512]{3,1,0,2:T(8,128)}, u32[]{:S(2)}) copy-start(f32[2,16,1,512]{3,1,0,2:T(8,128)} %copy-done.18) | copy-start | bytes 196612
  178.2 18.4 %copy-start.21 = (f32[2,16,1,512]{3,1,0,2:T(8,128)S(1)}, f32[2,16,1,512]{3,1,0,2:T(8,128)}, u32[]{:S(2)}) copy-start(f32[2,16,1,512]{3,1,0,2:T(8,128)} %copy-done.20) | copy-start | bytes 196612
